TPU v7x, 32 devices: a whole 2x2x4 slice. The times are simulated.
32 devices in a mesh: seq: 8 (over y, x, core), head: 4 (over z).
Axes of the slice: x: 2, y: 2, z: 4, core: 2. Of those that a mesh axis runs over, the one named last changes fastest.
Arguments:
- tokens: bfloat16 [4096, 5376], P('seq', 'head'), may hold values from -32 to 32
- query_weight: bfloat16 [5376, 4096], P(None, 'head'), may hold values from -1 to 1
- key_weight: bfloat16 [5376, 2048], P(None, 'head'), may hold values from -1 to 1
- value_weight: bfloat16 [5376, 2048], P(None, 'head'), may hold values from -0.078125 to 0.078125
- output_grad: bfloat16 [4096, 4096], P('seq', 'head'), may hold values from -48 to 48
- segments: int32 [4096], replicated, may hold values from 0 to 3, never falling along the last dimension, each value on 1 to 2048 neighbouring positions
Outputs:
- token_grad: bfloat16 [4096, 5376], P('seq', 'head')
- query_weight_grad: bfloat16 [5376, 4096], P('seq', 'head')
- key_weight_grad: bfloat16 [5376, 2048], P('seq', 'head')
- value_weight_grad: bfloat16 [5376, 2048], P('seq', 'head')
Inputs may be any that keep to these rules, and one draw needn't show every extreme that they name: `segments`: segment numbers never fall along the tokens; a segment has at most 2048 tokens.
All inputs are finite; a program needn't handle non-finite values.
Results may differ from a plain program's by a relative error of at most 0.015.
The roundings to bfloat16 on the way count: a program that leaves them out, or rounds other values in their place, can miss the bound.
Values may be sent and summed in bfloat16 or wider, within the bound.
No kernel may reach another device: no remote copies, remote signals or barrier semaphores. Data moves between devices by JAX's collectives and lax.ppermute only.
A program may use at most 192 MiB of HBM per device.

v0:
```python
import jax
import jax.numpy as jnp
from jax import lax
from jax.sharding import PartitionSpec as P

D = 5376
HEADS = 32
KV_HEADS = 16
HEAD_DIM = 128
WINDOW = 1024
HOPS = 2
neg_large = -1e30


def passed_along(x, axis, by):
    count = lax.axis_size(axis)
    pairs = [(i, i + by) for i in range(count) if 0 <= i + by < count]
    return lax.ppermute(x, axis, pairs)


def contract_last(left, right):
    return lax.dot_general(
        left, right, (((1,), (1,)), ((), ())), preferred_element_type=jnp.float32
    )


def contract_first(left, right):
    return lax.dot_general(
        left, right, (((0,), (0,)), ((), ())), preferred_element_type=jnp.float32
    )


def attend(queries, key_value, grads, query_first, key_first, seg_query, seg_key):
    tok_rows = queries.shape[0]
    key_rows = key_value.shape[1]
    groups = HEADS // KV_HEADS
    kv_local = key_value.shape[2] // HEAD_DIM
    score_scale = (D / HEADS) ** (-0.5)
    query_four = queries.reshape(tok_rows, kv_local, groups, HEAD_DIM)
    grad_four = grads.reshape(tok_rows, kv_local, groups, HEAD_DIM)
    key_three = key_value[0].reshape(key_rows, kv_local, HEAD_DIM)
    value_three = key_value[1].reshape(key_rows, kv_local, HEAD_DIM)
    query_pos = query_first + jnp.arange(tok_rows, dtype=jnp.int32)
    key_pos = key_first + jnp.arange(key_rows, dtype=jnp.int32)
    spacing = query_pos[:, None] - key_pos[None, :]
    allowed = (
        (key_pos >= 0)[None, :]
        & (spacing >= 0)
        & (spacing < WINDOW)
        & (seg_query[:, None] == seg_key[None, :])
    )
    scores = (
        jnp.einsum("akgd,ckd->kgac", query_four, key_three, preferred_element_type=jnp.float32)
        * score_scale
    )
    masked = jnp.where(allowed, scores, neg_large)
    row_max = jnp.max(masked, axis=-1, keepdims=True)
    expo = jnp.where(allowed, jnp.exp(masked - row_max), 0.0)
    probs = expo / jnp.sum(expo, axis=-1, keepdims=True)
    dprobs = jnp.einsum(
        "akgd,ckd->kgac", grad_four, value_three, preferred_element_type=jnp.float32
    )
    center = jnp.sum(probs * dprobs, axis=-1, keepdims=True)
    dscores = (probs * (dprobs - center)).astype(jnp.bfloat16)
    probs_low = probs.astype(jnp.bfloat16)
    query_grad = (
        (
            jnp.einsum("kgac,ckd->akgd", dscores, key_three, preferred_element_type=jnp.float32)
            * score_scale
        )
        .reshape(tok_rows, -1)
        .astype(jnp.bfloat16)
    )
    key_grad = (
        jnp.einsum("kgac,akgd->ckd", dscores, query_four, preferred_element_type=jnp.float32)
        * score_scale
    ).reshape(key_rows, -1)
    value_grad = jnp.einsum(
        "kgac,akgd->ckd", probs_low, grad_four, preferred_element_type=jnp.float32
    ).reshape(key_rows, -1)
    return (query_grad, jnp.stack([key_grad, value_grad]))


def per_device(tokens, query_weight, key_weight, value_weight, output_grad, segments):
    tok_rows = tokens.shape[0]
    hop_count = HOPS
    margin = hop_count * tok_rows
    gathered = lax.all_gather(tokens, "head", axis=1, tiled=True)
    queries = jnp.dot(gathered, query_weight, preferred_element_type=jnp.float32).astype(
        jnp.bfloat16
    )
    keys_own = jnp.dot(gathered, key_weight, preferred_element_type=jnp.float32).astype(
        jnp.bfloat16
    )
    values_own = jnp.dot(gathered, value_weight, preferred_element_type=jnp.float32).astype(
        jnp.bfloat16
    )
    key_value = jnp.stack([keys_own, values_own])
    blocks = [key_value] * (hop_count + 1)
    moving = key_value
    for distance in range(1, hop_count + 1):
        moving = passed_along(moving, "seq", 1)
        blocks[hop_count - distance] = moving
    keys_all = jnp.concatenate(blocks, axis=1)
    position = lax.axis_index("seq")
    query_first = position * tok_rows
    seg_query = lax.dynamic_slice_in_dim(segments, query_first, tok_rows, 0)
    seg_padded = jnp.concatenate([jnp.full((margin,), -1, jnp.int32), segments], axis=0)
    seg_key = lax.dynamic_slice_in_dim(seg_padded, query_first, (hop_count + 1) * tok_rows, 0)
    query_grad, kv_grad = attend(
        queries, keys_all, output_grad, query_first, query_first - margin, seg_query, seg_key
    )
    pieces = [
        kv_grad[:, block * tok_rows : (block + 1) * tok_rows] for block in range(hop_count + 1)
    ]
    carried = pieces[0]
    for distance in range(1, hop_count + 1):
        carried = pieces[distance] + passed_along(carried.astype(jnp.bfloat16), "seq", -1).astype(
            carried.dtype
        )
    key_grad = carried[0].astype(jnp.bfloat16)
    value_grad = carried[1].astype(jnp.bfloat16)
    partial_term = (
        contract_last(query_grad, query_weight)
        + contract_last(key_grad, key_weight)
        + contract_last(value_grad, value_weight)
    )
    token_grad = lax.psum_scatter(
        partial_term.astype(jnp.bfloat16), "head", scatter_dimension=1, tiled=True
    )
    proj_grads = jnp.concatenate([query_grad, key_grad, value_grad], axis=1)
    summed = lax.psum_scatter(
        contract_first(gathered, proj_grads).astype(jnp.bfloat16),
        "seq",
        scatter_dimension=0,
        tiled=True,
    ).astype(jnp.float32)
    summed = summed * (tok_rows * lax.axis_size("seq")) ** (-0.5)
    q_width = query_weight.shape[1]
    k_width = key_weight.shape[1]
    query_weight_grad = summed[:, :q_width].astype(jnp.bfloat16)
    key_weight_grad = summed[:, q_width : q_width + k_width].astype(jnp.bfloat16)
    value_weight_grad = summed[:, q_width + k_width :].astype(jnp.bfloat16)
    return (token_grad, query_weight_grad, key_weight_grad, value_weight_grad)


def solution(mesh):
    in_specs = (
        P("seq", "head"),
        P(None, "head"),
        P(None, "head"),
        P(None, "head"),
        P("seq", "head"),
        P(),
    )
    out_specs = (P("seq", "head"), P("seq", "head"), P("seq", "head"), P("seq", "head"))
    return jax.shard_map(
        per_device, mesh=mesh, in_specs=in_specs, out_specs=out_specs, check_vma=False
    )
```

profile of v0, /device:TPU:0, one launch (start us, length us, event | category | flops | bytes accessed | tf_op | source)
XLA Modules:
  0.0 569.0 jit_solution(12160398720478876539)
XLA Ops:
  7.2 0.0 all-gather.2.cloned.1.call-start
  7.2 0.7 all-gather.2.cloned.1.call-update
  7.9 0.0 reduce-scatter.7.cloned.1.call-start
  7.9 106.7 %all-gather.2.cloned.1.call-done = bf16[512,5376]{0,1:T(8,128)(2,1)} async-done(((bf16[512,1344]{0,1:T(8,128)(2,1)}), bf16[512,5376]{0,1:T(8,128)(2,1)}) %all-gather.2.cloned.1.call-update) | async-done | bytes 5505040 | tf_op jit(solution)/shard_map/all_gather | solution.py:88
  114.7 7.3 %fusion.32 = bf16[1,512,512]{2,1,0:T(8,128)(2,1)S(1)} fusion(bf16[512,5376]{0,1:T(8,128)(2,1)} %all-gather.2.cloned.1.call-done, bf16[5376,512]{1,0:T(8,128)(2,1)} %param.9), kind=kOutput, calls=%fused_computation.52 | convolution fusion | flops 2818834432 | bytes 11534336 | tf_op jit(solution)/shard_map/dot_general | solution.py:95
  122.0 0.0 copy-done.8
  122.1 0.0 copy-start.4
  122.1 0.0 copy-start.7
  122.1 5.7 fusion.31
  127.8 0.1 pad_maximum_fusion.1
  127.9 2.9 collective-permute-start
  130.8 0.0 copy-done.4
  130.8 1.3 copy.53
  132.1 0.0 copy-done.7
  132.1 0.1 dynamic_slice.6
  132.2 0.1 pad_dynamic-slice_fusion
  132.3 2.6 fusion.16
  134.9 0.0 collective-permute-done
  134.9 10.3 %collective-permute-start.1 = (bf16[2,512,512]{2,1,0:T(8,128)(2,1)}, bf16[2,512,512]{2,1,0:T(8,128)(2,1)S(1)}, u32[]{:S(2)}, u32[]{:S(2)}) collective-permute-start(bf16[2,512,512]{2,1,0:T(8,128)(2,1)} %collective-permute-done), channel_id=1, source_target_pairs={{0,4},{4,8},{8,12},{12,16},{16,20},{20,24},{24,28},{1,5},{5,9},{9,... | collective-permute-start | bytes 3145736 | tf_op jit(solution)/shard_map/ppermute | solution.py:18
  145.2 10.4 %convolution_convert_fusion.1 = bf16[512,1024]{1,0:T(8,128)(2,1)S(1)} fusion(bf16[512,5376]{0,1:T(8,128)(2,1)} %all-gather.2.cloned.1.call-done, bf16[5376,1024]{1,0:T(8,128)(2,1)} %param.7), kind=kOutput, calls=%fused_computation.48 | convolution fusion | flops 5637668864 | bytes 17563648 | tf_op jit(solution)/shard_map/dot_general | solution.py:89
  155.6 1.3 copy.52
  156.9 0.0 collective-permute-done.1
  156.9 1.4 maximum_maximum_fusion
  158.3 1.4 fusion.38
  159.7 0.4 reshape_squeeze.6
  160.1 1.0 copy.38
  161.1 0.0 copy-start.2
  161.1 2.8 reshape_squeeze.7
  163.9 17.4 %fusion.39 = (f32[4,2,512]{2,1,0:T(2,128)S(1)}, f32[4,2,512,1536]{2,3,1,0:T(8,128)}) fusion(pred[512,1536]{0,1:T(8,128)(4,1)} %fusion.16, bf16[1536,4,128,1]{0,2,3,1:T(8,128)(2,1)S(1)} %copy.38, bf16[512,4,2,128]{0,3,2,1:T(8,128)(2,1)} %bitcast.77), kind=kOutput, calls=%fused_computation.66 | convolution fusion | flops 1642071552 | bytes 28590080 | tf_op jit(solution)/shard_map/sub | solution.py:58
  181.2 0.0 copy-done.2
  181.3 0.0 copy-start.5
  181.3 12.5 %fusion.6 = f32[4,1536,128,1]{1,2,3,0:T(8,128)} fusion(bf16[512,4,2,128]{0,3,2,1:T(8,128)(2,1)} %bitcast.80, f32[4,2,512,1536]{2,3,1,0:T(8,128)} %get-tuple-element.19, f32[4,2,512]{2,1,0:T(2,128)S(1)} %get-tuple-element.18), kind=kOutput, calls=%fused_computation.11 | convolution fusion | flops 1623195648 | bytes 29376512 | tf_op jit(solution)/shard_map/kgac,akgd->ckd/dot_general | solution.py:78
  193.8 0.0 copy-done.5
  193.8 16.6 %fusion.1 = (f32[4,2,512]{2,1,0:T(2,128)S(1)}, f32[4,1536,512,2]{2,1,3,0:T(8,128)}) fusion(f32[4,2,512,1536]{2,3,1,0:T(8,128)} %get-tuple-element.19, f32[4,2,512]{2,1,0:T(2,128)S(1)} %get-tuple-element.18, bf16[512,4,2,128]{0,3,2,1:T(8,128)(2,1)S(1)} %bitcast.81, bf16[1536,4,128,1]{2,1,0,3:T(4,128)(2,1)S(1)} %bitcast.79), kind=kOutput, calls=%fused_computation.3 | convolution fusion | flops 1629483008 | bytes 52985856 | tf_op jit(solution)/shard_map/akgd,ckd->kgac/dot_general | solution.py:60
  210.4 16.8 %fusion.3 = bf16[4,2,512,1536]{2,3,1,0:T(8,128)(2,1)S(1)} fusion(f32[4,1536,512,2]{2,1,3,0:T(8,128)} %get-tuple-element.21, f32[4,2,512]{2,1,0:T(2,128)S(1)} %get-tuple-element.20, f32[4,2,512,1536]{2,3,1,0:T(8,128)} %get-tuple-element.19, f32[4,2,512]{2,1,0:T(2,128)S(1)} %get-tuple-element.18), kind=kLoop, calls=%fused_computation.5 | loop fusion | flops 25165824 | bytes 62947328 | tf_op jit(solution)/shard_map/convert_element_type | solution.py:64
  227.2 7.0 %fusion.13 = f32[4,128,1536]{2,1,0:T(8,128)} fusion(bf16[512,4,2,128]{0,3,2,1:T(8,128)(2,1)} %bitcast.78, bf16[4,2,512,1536]{2,3,1,0:T(8,128)(2,1)S(1)} %fusion.3), kind=kOutput, calls=%fused_computation.27 | convolution fusion | flops 1611399168 | bytes 16777216 | tf_op jit(solution)/shard_map/kgac,akgd->ckd/dot_general | solution.py:75
  234.2 1.8 fusion.23
  236.1 1.6 collective-permute-start.2
  237.7 5.4 collective-permute-done.2
  243.1 0.0 copy-done.1
  243.1 0.4 fusion.19
  243.5 1.3 collective-permute-start.3
  244.8 2.8 multiply_convert_fusion.1
  247.6 12.7 %collective-permute-done.3 = bf16[2,512,512]{1,2,0:T(8,128)(2,1)S(1)} collective-permute-done((bf16[2,512,512]{1,2,0:T(8,128)(2,1)S(1)}, bf16[2,512,512]{1,2,0:T(8,128)(2,1)S(1)}, u32[]{:S(2)}, u32[]{:S(2)}) %collective-permute-start.3) | collective-permute-done | bytes 1048608 | tf_op jit(solution)/shard_map/ppermute | solution.py:18
  260.2 0.4 fusion.22
  260.6 0.1 slice_bitcast_fusion.1
  260.7 0.0 copy-done.6
  260.7 20.0 %fusion.5 = bf16[5376,2048]{0,1:T(8,128)(2,1)} fusion(bf16[512,5376]{0,1:T(8,128)(2,1)} %all-gather.2.cloned.1.call-done, bf16[512,512]{0,1:T(8,128)(2,1)S(1)} %get-tuple-element.17, bf16[512,512]{0,1:T(8,128)(2,1)S(1)} %get-tuple-element.16, bf16[512,1024]{0,1:T(8,128)(2,1)S(1)} %bitcast.82), kind=kOutput, calls=%fused_computation.10 | convolution fusion | flops 11291590656 | bytes 29622272 | tf_op jit(solution)/shard_map/dot_general | solution.py:28
  280.7 28.2 %copy.50 = bf16[5376,2048]{1,0:T(8,128)(2,1)} copy(bf16[5376,2048]{0,1:T(8,128)(2,1)} %fusion.5) | data formatting | bytes 44040192
  308.9 0.0 reduce-scatter.7.cloned.1.call-update
  308.9 0.0 reduce-scatter.5.cloned.1.call-start
  309.0 13.0 %fusion.40 = f32[512,5376]{0,1:T(8,128)} fusion(bf16[5376,1024]{1,0:T(8,128)(2,1)} %param.7, bf16[512,1024]{0,1:T(8,128)(2,1)S(1)} %bitcast.83), kind=kOutput, calls=%fused_computation.67 | convolution fusion | flops 5637144576 | bytes 23068672 | tf_op jit(solution)/shard_map/dot_general | solution.py:22
  321.9 9.3 %fusion.36 = f32[512,5376]{0,1:T(8,128)} fusion(bf16[5376,512]{1,0:T(8,128)(2,1)} %param.8, bf16[2,512,512]{1,2,0:T(8,128)(2,1)S(1)} %fusion.22), kind=kOutput, calls=%fused_computation.63 | convolution fusion | flops 2818572288 | bytes 17039360 | tf_op jit(solution)/shard_map/dot_general | solution.py:22
  331.3 19.3 %add_convert_fusion = bf16[512,5376]{0,1:T(8,128)(2,1)} fusion(f32[512,5376]{0,1:T(8,128)} %fusion.40, f32[512,5376]{0,1:T(8,128)} %fusion.36, bf16[5376,512]{1,0:T(8,128)(2,1)} %param.9, bf16[2,512,512]{1,2,0:T(8,128)(2,1)S(1)} %fusion.22), kind=kOutput, calls=%fused_computation.17 | convolution fusion | flops 2826829824 | bytes 33554432 | tf_op jit(solution)/shard_map/dot_general | solution.py:22
  350.6 0.0 reduce-scatter.5.cloned.1.call-update
  350.6 111.0 %reduce-scatter.7.cloned.1.call-done = bf16[672,2048]{1,0:T(8,128)(2,1)} async-done(((bf16[5376,2048]{1,0:T(8,128)(2,1)}), bf16[672,2048]{1,0:T(8,128)(2,1)}) %reduce-scatter.7.cloned.1.call-update) | async-done | bytes 2752528
  461.6 4.6 copy.51
  466.2 2.5 multiply_convert_fusion
  468.7 1.3 slice.54
  469.9 2.9 copy.33
  472.9 1.3 fusion.37
  474.1 2.2 copy.34
  476.4 2.2 copy.35
  478.6 83.9 %reduce-scatter.5.cloned.1.call-done = bf16[512,1344]{0,1:T(8,128)(2,1)} async-done(((bf16[512,5376]{0,1:T(8,128)(2,1)}), bf16[512,1344]{0,1:T(8,128)(2,1)}) %reduce-scatter.5.cloned.1.call-update) | async-done | bytes 1376272 | tf_op jit(solution)/shard_map/reduce_scatter | solution.py:128
  (9 shorter events, 0.0 us)
Async XLA Ops:
  7.2 107.5 %all-gather.2.cloned.1.call-start = ((), (), s32[]{:S(2)}) async-start(), calls=%async_computation.2 | async-start | bytes 6881280 | tf_op jit(solution)/shard_map/all_gather | solution.py:88
  7.9 453.7 %reduce-scatter.7.cloned.1.call-start = ((), (), s32[]{:S(2)}) async-start(), calls=%async_computation.4 | async-start | bytes 24772608
  114.7 7.4 %copy-start.8 = (bf16[512,5376]{0,1:T(8,128)(2,1)S(1)}, bf16[512,5376]{0,1:T(8,128)(2,1)}, u32[]{:S(2)}) copy-start(bf16[512,5376]{0,1:T(8,128)(2,1)} %all-gather.2.cloned.1.call-done) | copy-start | bytes 16515076
  122.1 8.7 %copy-start.4 = (bf16[512,1024]{1,0:T(8,128)(2,1)S(1)}, bf16[512,1024]{1,0:T(8,128)(2,1)}, u32[]{:S(2)}) copy-start(bf16[512,1024]{1,0:T(8,128)(2,1)} %param.10) | copy-start | bytes 3145732
  122.1 10.0 %copy-start.7 = (s32[4096]{0:T(1024)S(1)}, s32[4096]{0:T(1024)}, u32[]{:S(2)}) copy-start(s32[4096]{0:T(1024)} %param.11) | copy-start | bytes 49156
  127.9 7.0 %collective-permute-start = (bf16[2,512,512]{2,1,0:T(8,128)(2,1)S(1)}, bf16[2,512,512]{2,1,0:T(8,128)(2,1)}, u32[]{:S(2)}, u32[]{:S(2)}) collective-permute-start(bf16[2,512,512]{2,1,0:T(8,128)(2,1)S(1)} %pad_maximum_fusion.1), channel_id=1, source_target_pairs={{0,4},{4,8},{8,12},{12,16},{16,20},{20,24},{24,28},{1,5},{5,9},{9,... | collective-permute-start | bytes 3145736 | tf_op jit(solution)/shard_map/ppermute | solution.py:18
  134.9 22.0 %collective-permute-start.1 = (bf16[2,512,512]{2,1,0:T(8,128)(2,1)}, bf16[2,512,512]{2,1,0:T(8,128)(2,1)S(1)}, u32[]{:S(2)}, u32[]{:S(2)}) collective-permute-start(bf16[2,512,512]{2,1,0:T(8,128)(2,1)} %collective-permute-done), channel_id=1, source_target_pairs={{0,4},{4,8},{8,12},{12,16},{16,20},{20,24},{24,28},{1,5},{5,9},{9,... | collective-permute-start | bytes 3145736 | tf_op jit(solution)/shard_map/ppermute | solution.py:18
  161.1 20.2 %copy-start.2 = (bf16[1536,4,128,1]{0,2,3,1:T(8,128)(2,1)}, bf16[1536,4,128,1]{0,2,3,1:T(8,128)(2,1)S(1)}, u32[]{:S(2)}) copy-start(bf16[1536,4,128,1]{0,2,3,1:T(8,128)(2,1)S(1)} %copy.38) | copy-start | bytes 4718596
  181.3 12.5 %copy-start.5 = (bf16[512,1024]{0,1:T(8,128)(2,1)S(1)}, bf16[512,1024]{0,1:T(8,128)(2,1)}, u32[]{:S(2)}) copy-start(bf16[512,1024]{0,1:T(8,128)(2,1)} %copy.53) | copy-start | bytes 3145732
  234.2 8.9 %copy-start = (f32[4,128,1536]{2,1,0:T(8,128)S(1)}, f32[4,128,1536]{2,1,0:T(8,128)}, u32[]{:S(2)}) copy-start(f32[4,128,1536]{2,1,0:T(8,128)} %fusion.13) | copy-start | bytes 9437188
  234.2 8.9 %copy-start.1 = (f32[4,1536,128,1]{1,2,3,0:T(8,128)S(1)}, f32[4,1536,128,1]{1,2,3,0:T(8,128)}, u32[]{:S(2)}) copy-start(f32[4,1536,128,1]{1,2,3,0:T(8,128)} %fusion.6) | copy-start | bytes 9437188
  236.1 8.7 %copy-start.3 = (bf16[1536,4,128,1]{0,2,3,1:T(8,128)(2,1)S(1)}, bf16[1536,4,128,1]{0,2,3,1:T(8,128)(2,1)}, u32[]{:S(2)}) copy-start(bf16[1536,4,128,1]{0,2,3,1:T(8,128)(2,1)} %copy-done.2) | copy-start | bytes 4718596
  236.1 7.0 %collective-permute-start.2 = (bf16[2,512,512]{1,2,0:T(8,128)(2,1)S(1)}, bf16[2,512,512]{1,2,0:T(8,128)(2,1)S(1)}, u32[]{:S(2)}, u32[]{:S(2)}) collective-permute-start(bf16[2,512,512]{1,2,0:T(8,128)(2,1)S(1)} %fusion.23), channel_id=1, source_target_pairs={{4,0},{8,4},{12,8},{16,12},{20,16},{24,20},{28,24},{5,1},{9,5},{13... | collective-permute-start | bytes 3145736 | tf_op jit(solution)/shard_map/ppermute | solution.py:18
  243.5 16.8 %collective-permute-start.3 = (bf16[2,512,512]{1,2,0:T(8,128)(2,1)S(1)}, bf16[2,512,512]{1,2,0:T(8,128)(2,1)S(1)}, u32[]{:S(2)}, u32[]{:S(2)}) collective-permute-start(bf16[2,512,512]{1,2,0:T(8,128)(2,1)S(1)} %fusion.19), channel_id=1, source_target_pairs={{4,0},{8,4},{12,8},{16,12},{20,16},{24,20},{28,24},{5,1},{9,5},{13... | collective-permute-start | bytes 3145736 | tf_op jit(solution)/shard_map/ppermute | solution.py:18
  247.6 13.1 %copy-start.6 = (bf16[4,128,2,512]{3,1,2,0:T(8,128)(2,1)S(1)}, bf16[4,128,2,512]{3,1,2,0:T(8,128)(2,1)}, u32[]{:S(2)}) copy-start(bf16[4,128,2,512]{3,1,2,0:T(8,128)(2,1)} %multiply_convert_fusion.1) | copy-start | bytes 3145732
  308.9 253.6 %reduce-scatter.5.cloned.1.call-start = ((), (), s32[]{:S(2)}) async-start(), calls=%async_computation.3 | async-start | bytes 6881280 | tf_op jit(solution)/shard_map/reduce_scatter | solution.py:128
Sparse Core Ops, SparseCore 0:
  9.6 105.0 all-gather.1
  309.0 152.5 reduce-scatter.6
  464.5 97.9 reduce-scatter.4
where the time goes:
time: 570 us; the launch traced here: 569 us
  waiting for transfers between devices  320 us (56%)
  matrix products  141 us (25%)
  local copies, waits for them, and re-layouts  51.1 us (9%)
  other arithmetic  26 us (5%)
  starting transfers between devices  16.2 us (3%)
  between operations  14 us (2%)
    unnamed x4, waiting for transfers between devices  112 us
    all_gather x1, waiting for transfers between devices, per_device(): gathered = lax.all_gather(tokens, 'head', axis=1, tiled=True)  107 us
    reduce_scatter x1, waiting for transfers between devices, per_device(): lax.psum_scatter(partial_term.astype(jnp.bfloat16), 'head', scatter_dimen...  83.9 us
    dot_general x3, matrix products, contract_last(): lax.dot_general(left, right, (((1,), (1,)), ((), ())), preferred_element_...  41.6 us
    unnamed x23, local copies, waits for them, and re-layouts  40.2 us
    dot_general x1, matrix products, contract_first(): lax.dot_general(left, right, (((0,), (0,)), ((), ())), preferred_element_...  20 us
    ppermute x4, waiting for transfers between devices, passed_along(): return lax.ppermute(x, axis, pairs)  18.1 us
    sub x1, matrix products, attend(): expo = jnp.where(allowed, jnp.exp(masked - row_max), 0.0)  17.4 us
  transfers between devices with their start and end apart: 7, of which 5 were waited for; matrix products, arithmetic and copies ran while one was open for 14% of the time, Pallas kernels for 0%

commit v1 on v0

--- a/solution.py
+++ b/solution.py
@@ -10,6 +10,22 @@
 WINDOW = 1024
 HOPS = 2
 neg_large = -1e30
+
+
+def _manage_clusters(target, axis_key):
+    n_blocks = lax.axis_size(axis_key)
+    arrivals = tuple(((w, (w + 1) % n_blocks) for w in range(n_blocks)))
+    chunks = tuple(((w, (w - 1) % n_blocks) for w in range(n_blocks)))
+    reached, latest = ([target], [target])
+    for _ in range(n_blocks // 2):
+        reached.append(lax.ppermute(reached[-1], axis_key, arrivals))
+    for _ in range((n_blocks - 1) // 2):
+        latest.append(lax.ppermute(latest[-1], axis_key, chunks))
+    response = jnp.concatenate([*reached[::-1], *latest[1:]], axis=1)
+    taken_in = jnp.roll(
+        response, shift=(lax.axis_index(axis_key) - n_blocks // 2) * target.shape[1], axis=1
+    )
+    return taken_in
 
 
 def passed_along(x, axis, by):
@@ -85,7 +101,7 @@
     tok_rows = tokens.shape[0]
     hop_count = HOPS
     margin = hop_count * tok_rows
-    gathered = lax.all_gather(tokens, "head", axis=1, tiled=True)
+    gathered = _manage_clusters(tokens, "head")
     queries = jnp.dot(gathered, query_weight, preferred_element_type=jnp.float32).astype(
         jnp.bfloat16
     )

time: 570 us -> 538 us (0.944)
  local copies, waits for them, and re-layouts: 51.1 us -> 18.6 us
  starting transfers between devices: 16.2 us -> 23.1 us
  waiting for transfers between devices: 320 us -> 314 us
    reduce_scatter x0 -> x1, waiting for transfers between devices: none -> 112 us  [per_device(): lax.psum_scatter(contract_first(gathered, proj_grads).astype(jnp.bfloat16...]
    unnamed x4 -> x2, waiting for transfers between devices: 112 us -> 0.03 us
    all_gather x1 -> x0, waiting for transfers between devices: 107 us -> none  [per_device(): gathered = lax.all_gather(tokens, 'head', axis=1, tiled=True)]
    ppermute x0 -> x3, waiting for transfers between devices: none -> 88.1 us  [the longest x2 63.6 us: _manage_clusters(): reached.append(lax.ppermute(reached[-1], axis_key, arrivals))]
    unnamed x23 -> x35, local copies, waits for them, and re-layouts: 40.2 us -> 6.24 us
    reduce_scatter x1, waiting for transfers between devices: 83.9 us -> 96.1 us  [per_device(): lax.psum_scatter(partial_term.astype(jnp.bfloat16), 'head', scatter_dimen...]
    ppermute x0 -> x3, starting transfers between devices: none -> 6.9 us  [the longest x1 3.82 us: _manage_clusters(): latest.append(lax.ppermute(latest[-1], axis_key, chunks))]
  transfers between devices with their start and end apart: 7 -> 9, of which waited for: 5 -> 7; matrix products, arithmetic and copies ran while one was open for 14% -> 13% of each run, Pallas kernels for 0% -> 0%
where the time goes in v1:
time: 538 us; the launch traced here: 532 us
  waiting for transfers between devices  314 us (58%)
  matrix products  136 us (25%)
  other arithmetic  25.9 us (5%)
  starting transfers between devices  23.1 us (4%)
  local copies, waits for them, and re-layouts  18.6 us (3%)
  between operations  14.6 us (3%)
    reduce_scatter x1, waiting for transfers between devices, per_device(): lax.psum_scatter(contract_first(gathered, proj_grads).astype(jnp.bfloat16...  112 us
    reduce_scatter x1, waiting for transfers between devices, per_device(): lax.psum_scatter(partial_term.astype(jnp.bfloat16), 'head', scatter_dimen...  96.1 us
    ppermute x2, waiting for transfers between devices, _manage_clusters(): reached.append(lax.ppermute(reached[-1], axis_key, arrivals))  63.6 us
    dot_general x3, matrix products, contract_last(): lax.dot_general(left, right, (((1,), (1,)), ((), ())), preferred_element_...  41.8 us
    ppermute x1, waiting for transfers between devices, _manage_clusters(): latest.append(lax.ppermute(latest[-1], axis_key, chunks))  24.5 us
    dot_general x1, matrix products, contract_first(): lax.dot_general(left, right, (((0,), (0,)), ((), ())), preferred_element_...  20.3 us
    sub x1, matrix products, attend(): expo = jnp.where(allowed, jnp.exp(masked - row_max), 0.0)  17.5 us
    ppermute x4, waiting for transfers between devices, passed_along(): return lax.ppermute(x, axis, pairs)  17.3 us
  transfers between devices with their start and end apart: 9, of which 7 were waited for; matrix products, arithmetic and copies ran while one was open for 13% of the time, Pallas kernels for 0%

profile of v1, /device:TPU:0, one launch (start us, length us, event | category | flops | bytes accessed | tf_op | source)
XLA Modules:
  0.0 531.8 jit_solution(1486726317921719031)
XLA Ops:
  7.2 0.0 reduce-scatter.5.cloned.1.call-start
  7.2 3.1 collective-permute-start
  10.3 32.4 %collective-permute-done = bf16[512,1344]{0,1:T(8,128)(2,1)S(1)} collective-permute-done((bf16[512,1344]{0,1:T(8,128)(2,1)}, bf16[512,1344]{0,1:T(8,128)(2,1)S(1)}, u32[]{:S(2)}, u32[]{:S(2)}) %collective-permute-start) | collective-permute-done | bytes 1376288 | tf_op jit(solution)/shard_map/ppermute | solution.py:21
  42.7 0.0 collective-permute-start.1
  42.7 3.8 collective-permute-start.2
  46.5 31.2 %collective-permute-done.1 = bf16[512,1344]{0,1:T(8,128)(2,1)} collective-permute-done((bf16[512,1344]{0,1:T(8,128)(2,1)S(1)}, bf16[512,1344]{0,1:T(8,128)(2,1)}, u32[]{:S(2)}, u32[]{:S(2)}) %collective-permute-start.1) | collective-permute-done | bytes 1376288 | tf_op jit(solution)/shard_map/ppermute | solution.py:21
  77.7 1.4 constant_dynamic-update-slice_fusion.7
  79.2 0.1 constant_dynamic-update-slice_fusion.6
  79.3 0.1 constant_dynamic-update-slice_fusion.5
  79.4 24.5 %collective-permute-done.2 = bf16[512,1344]{0,1:T(8,128)(2,1)} collective-permute-done((bf16[512,1344]{0,1:T(8,128)(2,1)}, bf16[512,1344]{0,1:T(8,128)(2,1)}, u32[]{:S(2)}, u32[]{:S(2)}) %collective-permute-start.2) | collective-permute-done | bytes 1376288 | tf_op jit(solution)/shard_map/ppermute | solution.py:23
  103.9 1.6 constant_dynamic-update-slice_fusion.4
  105.5 1.5 constant_dynamic-update-slice_fusion.3
  107.0 0.0 slice-start.1
  107.0 0.1 constant_dynamic-update-slice_fusion.2
  107.1 0.1 constant_dynamic-update-slice_fusion.1
  107.2 0.0 slice-start.2
  107.2 1.6 constant_dynamic-update-slice_fusion
  108.8 0.0 slice-start.3
  108.9 3.0 fusion.46
  111.9 1.3 copy-done.8
  113.2 0.0 copy-start.9
  113.2 3.0 fusion.49
  116.3 0.1 pad_maximum_fusion.1
  116.4 2.3 collective-permute-start.3
  118.7 1.3 copy.35
  120.0 0.1 dynamic_slice.11
  120.1 0.1 pad_dynamic-slice_fusion
  120.2 2.6 fusion.22
  122.8 0.0 collective-permute-done.3
  122.8 11.0 %collective-permute-start.4 = (bf16[2,512,512]{2,1,0:T(8,128)(2,1)}, bf16[2,512,512]{2,1,0:T(8,128)(2,1)S(1)}, u32[]{:S(2)}, u32[]{:S(2)}) collective-permute-start(bf16[2,512,512]{2,1,0:T(8,128)(2,1)} %collective-permute-done.3), channel_id=1, source_target_pairs={{0,4},{4,8},{8,12},{12,16},{16,20},{20,24},{24,28},{1,5},{5,9},{9,... | collective-permute-start | bytes 3145736 | tf_op jit(solution)/shard_map/ppermute | solution.py:34
  133.8 11.1 %fusion.37 = bf16[512,1024]{1,0:T(8,128)(2,1)S(1)} fusion(bf16[5376,1024]{1,0:T(8,128)(2,1)} %param.7, bf16[512,10752]{0,1:T(8,128)(2,1)} %copy-done.8, s32[]{:T(128)S(6)} %select_n.27), kind=kOutput, calls=%fused_computation.54 | convolution fusion | flops 5637668864 | bytes 17563652 | tf_op jit(solution)/shard_map/dot_general | solution.py:105
  144.9 1.3 copy.34
  146.2 1.4 maximum_maximum_fusion
  147.6 1.4 fusion.60
  149.0 0.4 reshape_squeeze.6
  149.4 1.0 copy.22
  150.4 2.8 reshape_squeeze.7
  153.1 17.5 %fusion.62 = (f32[4,2,512]{2,1,0:T(2,128)S(1)}, f32[4,2,512,1536]{2,3,1,0:T(8,128)}) fusion(pred[512,1536]{0,1:T(8,128)(4,1)} %fusion.22, bf16[1536,4,128,1]{0,2,3,1:T(8,128)(2,1)S(1)} %copy.22, bf16[512,4,2,128]{0,3,2,1:T(8,128)(2,1)} %bitcast.74), kind=kOutput, calls=%fused_computation.84 | convolution fusion | flops 1642071552 | bytes 28590080 | tf_op jit(solution)/shard_map/sub | solution.py:74
  170.7 0.0 copy-start.6
  170.7 12.6 %fusion.5 = f32[4,1536,128,1]{1,2,3,0:T(8,128)} fusion(bf16[512,4,2,128]{0,3,2,1:T(8,128)(2,1)} %bitcast.77, f32[4,2,512,1536]{2,3,1,0:T(8,128)} %get-tuple-element.11, f32[4,2,512]{2,1,0:T(2,128)S(1)} %get-tuple-element.10), kind=kOutput, calls=%fused_computation.10 | convolution fusion | flops 1623195648 | bytes 29376512 | tf_op jit(solution)/shard_map/kgac,akgd->ckd/dot_general | solution.py:94
  183.3 16.6 %fusion.1 = (f32[4,2,512]{2,1,0:T(2,128)S(1)}, f32[4,1536,512,2]{2,1,3,0:T(8,128)}) fusion(f32[4,2,512,1536]{2,3,1,0:T(8,128)} %get-tuple-element.11, f32[4,2,512]{2,1,0:T(2,128)S(1)} %get-tuple-element.10, bf16[512,4,2,128]{0,3,2,1:T(8,128)(2,1)S(1)} %bitcast.78, bf16[1536,4,128,1]{2,1,0,3:T(4,128)(2,1)S(1)} %bitcast.76), kind=kOutput, calls=%fused_computation.3 | convolution fusion | flops 1629483008 | bytes 52985856 | tf_op jit(solution)/shard_map/akgd,ckd->kgac/dot_general | solution.py:76
  199.9 16.8 %fusion.3 = bf16[4,2,512,1536]{2,3,1,0:T(8,128)(2,1)S(1)} fusion(f32[4,1536,512,2]{2,1,3,0:T(8,128)} %get-tuple-element.13, f32[4,2,512]{2,1,0:T(2,128)S(1)} %get-tuple-element.12, f32[4,2,512,1536]{2,3,1,0:T(8,128)} %get-tuple-element.11, f32[4,2,512]{2,1,0:T(2,128)S(1)} %get-tuple-element.10), kind=kLoop, calls=%fused_computation.5 | loop fusion | flops 25165824 | bytes 62947328 | tf_op jit(solution)/shard_map/convert_element_type | solution.py:80
  216.7 7.0 %fusion.19 = f32[4,128,1536]{2,1,0:T(8,128)} fusion(bf16[512,4,2,128]{0,3,2,1:T(8,128)(2,1)} %bitcast.75, bf16[4,2,512,1536]{2,3,1,0:T(8,128)(2,1)S(1)} %fusion.3), kind=kOutput, calls=%fused_computation.33 | convolution fusion | flops 1611399168 | bytes 16777216 | tf_op jit(solution)/shard_map/kgac,akgd->ckd/dot_general | solution.py:91
  223.8 1.8 fusion.29
  225.6 1.6 collective-permute-start.5
  227.2 5.3 collective-permute-done.5
  232.4 0.4 fusion.25
  232.8 1.3 collective-permute-start.6
  234.1 2.8 multiply_convert_fusion.1
  236.9 12.0 %collective-permute-done.6 = bf16[2,512,512]{1,2,0:T(8,128)(2,1)S(1)} collective-permute-done((bf16[2,512,512]{1,2,0:T(8,128)(2,1)S(1)}, bf16[2,512,512]{1,2,0:T(8,128)(2,1)S(1)}, u32[]{:S(2)}, u32[]{:S(2)}) %collective-permute-start.6) | collective-permute-done | bytes 1048608 | tf_op jit(solution)/shard_map/ppermute | solution.py:34
  248.9 0.4 fusion.28
  249.3 0.1 slice_bitcast_fusion.1
  249.4 20.3 %convolution_convert_fusion = bf16[5376,2048]{1,0:T(8,128)(2,1)} fusion(bf16[512,10752]{0,1:T(8,128)(2,1)} %copy-done.8, s32[]{:T(128)S(6)} %select_n.27, bf16[512,512]{0,1:T(8,128)(2,1)S(1)} %get-tuple-element.9, bf16[512,512]{0,1:T(8,128)(2,1)S(1)} %get-tuple-element.8, bf16[512,1024]{0,1:T(8,128)(2,1)S(1)} %bitcast.79), kind=kOutput, calls=%fused_computation.8 | convolution fusion | flops 11291590656 | bytes 29622276 | tf_op jit(solution)/shard_map/dot_general | solution.py:44
  269.7 0.0 reduce-scatter.5.cloned.1.call-update
  269.7 0.0 reduce-scatter.3.cloned.1.call-start
  269.8 12.9 %fusion.63 = f32[512,5376]{0,1:T(8,128)} fusion(bf16[5376,1024]{1,0:T(8,128)(2,1)} %param.7, bf16[512,1024]{0,1:T(8,128)(2,1)S(1)} %bitcast.80), kind=kOutput, calls=%fused_computation.85 | convolution fusion | flops 5637144576 | bytes 23068672 | tf_op jit(solution)/shard_map/dot_general | solution.py:38
  282.7 9.4 %fusion.59 = f32[512,5376]{0,1:T(8,128)} fusion(bf16[5376,512]{1,0:T(8,128)(2,1)} %param.8, bf16[2,512,512]{1,2,0:T(8,128)(2,1)S(1)} %fusion.28), kind=kOutput, calls=%fused_computation.81 | convolution fusion | flops 2818572288 | bytes 17039360 | tf_op jit(solution)/shard_map/dot_general | solution.py:38
  292.1 19.4 %add_convert_fusion = bf16[512,5376]{0,1:T(8,128)(2,1)} fusion(f32[512,5376]{0,1:T(8,128)} %fusion.63, f32[512,5376]{0,1:T(8,128)} %fusion.59, bf16[5376,512]{1,0:T(8,128)(2,1)} %param.9, bf16[2,512,512]{1,2,0:T(8,128)(2,1)S(1)} %fusion.28), kind=kOutput, calls=%fused_computation.16 | convolution fusion | flops 2826829824 | bytes 33554432 | tf_op jit(solution)/shard_map/dot_general | solution.py:38
  311.5 0.0 reduce-scatter.3.cloned.1.call-update
  311.6 112.3 %reduce-scatter.5.cloned.1.call-done = bf16[672,2048]{1,0:T(8,128)(2,1)} async-done(((bf16[5376,2048]{1,0:T(8,128)(2,1)}), bf16[672,2048]{1,0:T(8,128)(2,1)}) %reduce-scatter.5.cloned.1.call-update) | async-done | bytes 2752528 | tf_op jit(solution)/shard_map/reduce_scatter | solution.py:148
  423.8 2.4 multiply_convert_fusion
  426.2 1.2 slice.54
  427.5 1.2 fusion.61
  428.7 96.1 %reduce-scatter.3.cloned.1.call-done = bf16[512,1344]{0,1:T(8,128)(2,1)} async-done(((bf16[512,5376]{0,1:T(8,128)(2,1)}), bf16[512,1344]{0,1:T(8,128)(2,1)}) %reduce-scatter.3.cloned.1.call-update) | async-done | bytes 1376272 | tf_op jit(solution)/shard_map/reduce_scatter | solution.py:144
  (27 shorter events, 0.1 us)
Async XLA Ops:
  7.2 72.1 %copy-start.4 = (bf16[512,1344]{0,1:T(8,128)(2,1)S(1)}, bf16[512,1344]{0,1:T(8,128)(2,1)}, u32[]{:S(2)}) copy-start(bf16[512,1344]{0,1:T(8,128)(2,1)} %param.6) | copy-start | bytes 4128772
  7.2 416.7 %reduce-scatter.5.cloned.1.call-start = ((), (), s32[]{:S(2)}) async-start(), calls=%async_computation.3 | async-start | bytes 24772608 | tf_op jit(solution)/shard_map/reduce_scatter | solution.py:148
  7.2 35.5 %collective-permute-start = (bf16[512,1344]{0,1:T(8,128)(2,1)}, bf16[512,1344]{0,1:T(8,128)(2,1)S(1)}, u32[]{:S(2)}, u32[]{:S(2)}) collective-permute-start(bf16[512,1344]{0,1:T(8,128)(2,1)} %param.6), channel_id=1, source_target_pairs={{0,1},{1,2},{2,3},{3,0},{4,5},{5,6},{6,7},{7,4},{8,9},{9,10},{10,1... | collective-permute-start | bytes 4128776 | tf_op jit(solution)/shard_map/ppermute | solution.py:21
  42.7 35.0 %collective-permute-start.1 = (bf16[512,1344]{0,1:T(8,128)(2,1)S(1)}, bf16[512,1344]{0,1:T(8,128)(2,1)}, u32[]{:S(2)}, u32[]{:S(2)}) collective-permute-start(bf16[512,1344]{0,1:T(8,128)(2,1)S(1)} %collective-permute-done), channel_id=1, source_target_pairs={{0,1},{1,2},{2,3},{3,0},{4,5},{5,6},{6,7},{7,4},{8,9},{9,10},{10,1... | collective-permute-start | bytes 4128776 | tf_op jit(solution)/shard_map/ppermute | solution.py:21
  42.7 61.2 %collective-permute-start.2 = (bf16[512,1344]{0,1:T(8,128)(2,1)}, bf16[512,1344]{0,1:T(8,128)(2,1)}, u32[]{:S(2)}, u32[]{:S(2)}) collective-permute-start(bf16[512,1344]{0,1:T(8,128)(2,1)} %param.6), channel_id=1, source_target_pairs={{0,3},{1,0},{2,1},{3,2},{4,7},{5,4},{6,5},{7,6},{8,11},{9,8},{10,9... | collective-permute-start | bytes 4128776 | tf_op jit(solution)/shard_map/ppermute | solution.py:23
  103.9 4.9 slice-start
  107.0 1.8 slice-start.1
  107.2 6.0 %slice-start.2 = ((s8[5505024]{0:T(1024)(128)(4,1)}), s8[4194304]{0:T(1024)(128)(4,1)S(1)}, s32[]{:S(2)}) async-start(s8[5505024]{0:T(1024)(128)(4,1)} %bitcast.71), calls=%async_computation.6 | async-start | bytes 8388608
  108.8 4.4 copy-start.8
  108.8 4.3 slice-start.3
  113.2 5.5 %copy-start.5 = (bf16[512,1024]{1,0:T(8,128)(2,1)S(1)}, bf16[512,1024]{1,0:T(8,128)(2,1)}, u32[]{:S(2)}) copy-start(bf16[512,1024]{1,0:T(8,128)(2,1)} %param.10) | copy-start | bytes 3145732
  113.2 6.8 %copy-start.9 = (s32[4096]{0:T(1024)S(1)}, s32[4096]{0:T(1024)}, u32[]{:S(2)}) copy-start(s32[4096]{0:T(1024)} %param.11) | copy-start | bytes 49156
  116.4 6.4 %collective-permute-start.3 = (bf16[2,512,512]{2,1,0:T(8,128)(2,1)S(1)}, bf16[2,512,512]{2,1,0:T(8,128)(2,1)}, u32[]{:S(2)}, u32[]{:S(2)}) collective-permute-start(bf16[2,512,512]{2,1,0:T(8,128)(2,1)S(1)} %pad_maximum_fusion.1), channel_id=1, source_target_pairs={{0,4},{4,8},{8,12},{12,16},{16,20},{20,24},{24,28},{1,5},{5,9},{9,... | collective-permute-start | bytes 3145736 | tf_op jit(solution)/shard_map/ppermute | solution.py:34
  122.8 23.5 %collective-permute-start.4 = (bf16[2,512,512]{2,1,0:T(8,128)(2,1)}, bf16[2,512,512]{2,1,0:T(8,128)(2,1)S(1)}, u32[]{:S(2)}, u32[]{:S(2)}) collective-permute-start(bf16[2,512,512]{2,1,0:T(8,128)(2,1)} %collective-permute-done.3), channel_id=1, source_target_pairs={{0,4},{4,8},{8,12},{12,16},{16,20},{20,24},{24,28},{1,5},{5,9},{9,... | collective-permute-start | bytes 3145736 | tf_op jit(solution)/shard_map/ppermute | solution.py:34
  150.4 20.3 %copy-start.2 = (bf16[1536,4,128,1]{0,2,3,1:T(8,128)(2,1)}, bf16[1536,4,128,1]{0,2,3,1:T(8,128)(2,1)S(1)}, u32[]{:S(2)}) copy-start(bf16[1536,4,128,1]{0,2,3,1:T(8,128)(2,1)S(1)} %copy.22) | copy-start | bytes 4718596
  170.7 12.6 %copy-start.6 = (bf16[512,1024]{0,1:T(8,128)(2,1)S(1)}, bf16[512,1024]{0,1:T(8,128)(2,1)}, u32[]{:S(2)}) copy-start(bf16[512,1024]{0,1:T(8,128)(2,1)} %copy.35) | copy-start | bytes 3145732
  223.8 8.7 %copy-start = (f32[4,128,1536]{2,1,0:T(8,128)S(1)}, f32[4,128,1536]{2,1,0:T(8,128)}, u32[]{:S(2)}) copy-start(f32[4,128,1536]{2,1,0:T(8,128)} %fusion.19) | copy-start | bytes 9437188
  223.8 8.7 %copy-start.1 = (f32[4,1536,128,1]{1,2,3,0:T(8,128)S(1)}, f32[4,1536,128,1]{1,2,3,0:T(8,128)}, u32[]{:S(2)}) copy-start(f32[4,1536,128,1]{1,2,3,0:T(8,128)} %fusion.5) | copy-start | bytes 9437188
  225.6 8.5 %copy-start.3 = (bf16[1536,4,128,1]{0,2,3,1:T(8,128)(2,1)S(1)}, bf16[1536,4,128,1]{0,2,3,1:T(8,128)(2,1)}, u32[]{:S(2)}) copy-start(bf16[1536,4,128,1]{0,2,3,1:T(8,128)(2,1)} %copy-done.2) | copy-start | bytes 4718596
  225.6 6.8 %collective-permute-start.5 = (bf16[2,512,512]{1,2,0:T(8,128)(2,1)S(1)}, bf16[2,512,512]{1,2,0:T(8,128)(2,1)S(1)}, u32[]{:S(2)}, u32[]{:S(2)}) collective-permute-start(bf16[2,512,512]{1,2,0:T(8,128)(2,1)S(1)} %fusion.29), channel_id=1, source_target_pairs={{4,0},{8,4},{12,8},{16,12},{20,16},{24,20},{28,24},{5,1},{9,5},{13... | collective-permute-start | bytes 3145736 | tf_op jit(solution)/shard_map/ppermute | solution.py:34
  232.8 16.1 %collective-permute-start.6 = (bf16[2,512,512]{1,2,0:T(8,128)(2,1)S(1)}, bf16[2,512,512]{1,2,0:T(8,128)(2,1)S(1)}, u32[]{:S(2)}, u32[]{:S(2)}) collective-permute-start(bf16[2,512,512]{1,2,0:T(8,128)(2,1)S(1)} %fusion.25), channel_id=1, source_target_pairs={{4,0},{8,4},{12,8},{16,12},{20,16},{24,20},{28,24},{5,1},{9,5},{13... | collective-permute-start | bytes 3145736 | tf_op jit(solution)/shard_map/ppermute | solution.py:34
  236.9 12.5 %copy-start.7 = (bf16[4,128,2,512]{3,1,2,0:T(8,128)(2,1)S(1)}, bf16[4,128,2,512]{3,1,2,0:T(8,128)(2,1)}, u32[]{:S(2)}) copy-start(bf16[4,128,2,512]{3,1,2,0:T(8,128)(2,1)} %multiply_convert_fusion.1) | copy-start | bytes 3145732
  269.7 255.0 %reduce-scatter.3.cloned.1.call-start = ((), (), s32[]{:S(2)}) async-start(), calls=%async_computation.2 | async-start | bytes 6881280 | tf_op jit(solution)/shard_map/reduce_scatter | solution.py:144
Sparse Core Ops, SparseCore 0:
  269.8 153.9 reduce-scatter.4
  426.7 97.9 reduce-scatter.2
